TPU v7x, 32 devices: a whole 2x2x4 slice. The times are simulated.
32 devices in a mesh: lon: 4 (over x, core), lat: 8 (over z, y).
Axes of the slice: x: 2, y: 2, z: 4, core: 2. Of those that a mesh axis runs over, the one named last changes fastest.
Arguments:
- prognostic: float32 [4, 16, 192, 1536], P(None, None, 'lat', 'lon'), may hold values from -6 to 6
- tracers: float32 [4, 16, 192, 1536], P(None, None, 'lat', 'lon'), may hold values from -6 to 6
- zonal_courant: float32 [16, 192, 1536], P(None, 'lat', 'lon'), may hold values from -0.45 to 0.45
- meridional_courant: float32 [16, 192, 1536], P(None, 'lat', 'lon'), may hold values from -0.45 to 0.45
- filter_band: int32 [192], P('lat'), may hold values from 96 to 768, as said below
- dep_owner: int32 [192, 2], P('lat'), may hold values from 0 to 7, as said below
- dep_row: int32 [192, 2], P('lat'), may hold values from 0 to 23
- dep_weight: float32 [192, 2], P('lat'), may hold values from 0 to 1, as said below
Outputs:
- new_prognostic: float32 [4, 16, 192, 1536], P(None, None, 'lat', 'lon')
- new_tracers: float32 [4, 16, 192, 1536], P(None, None, 'lat', 'lon')
Inputs may be any that keep to these rules, and one draw needn't show every extreme that they name: `filter_band`: rows within 24 of either pole hold values below 768; all other rows hold 768. `dep_owner`: among the 48 entries of one band, at most 12 name the same owner band, and some owner is named exactly 12 times; the owners a band names are the bands nearest to it, distance counted across either pole. `dep_weight`: Positive; the 2 weights of a row sum to 1.
All inputs are finite; a program needn't handle non-finite values.
Results may differ from a plain program's by a relative error of at most 0.00007.
Values sent between devices are 32-bit elements; how exact they have to be, the bound alone decides.
No kernel may reach another device: no remote copies, remote signals or barrier semaphores. Data moves between devices by JAX's collectives and lax.ppermute only.
A program may use at most 128 MiB of HBM per device.

v0:
```python
import math
import jax
import jax.numpy as jnp
from jax import lax
from jax.sharding import PartitionSpec as P

PRECISE = lax.Precision.HIGHEST


def padded(value, sides, width, wrap):
    for axis, dim in sides:
        size, length = (lax.axis_size(axis), value.shape[dim])
        up = [(i, (i + 1) % size) for i in range(size if wrap else size - 1)]
        down = [(j, i) for i, j in up]
        last = lax.slice_in_dim(value, length - width, length, axis=dim)
        first = lax.slice_in_dim(value, 0, width, axis=dim)
        before = lax.ppermute(last, axis, up)
        after = lax.ppermute(first, axis, down)
        value = jnp.concatenate([before, value, after], axis=dim)
    return value


def face_flux(values, speeds, axis):
    count = values.shape[axis] - 2
    left_cells = lax.slice_in_dim(values, 0, count + 1, axis=axis)
    right_cells = lax.slice_in_dim(values, 1, count + 2, axis=axis)
    courant = lax.slice_in_dim(speeds, 0, count + 1, axis=axis)
    return 0.5 * courant * (left_cells + right_cells) - 0.5 * courant * courant * (
        right_cells - left_cells
    )


def column_factors(band_rows, length):
    column = jnp.arange(length, dtype=jnp.int32)
    half_length = length // 2
    frequency = jnp.where(column <= half_length, column, column - half_length)
    single = (column == 0) | (column == half_length)
    weights = jnp.where(single, 1.0 / length, 2.0 / length).astype(jnp.float32)
    ratios = (
        band_rows.astype(jnp.float32)[:, None]
        / jnp.maximum(frequency, 1).astype(jnp.float32)[None, :]
    )
    damping = jnp.minimum(1.0, ratios * ratios)
    return (damping - 1.0) * weights[None, :]


def circle_basis(length):
    half_length = length // 2
    column = jnp.arange(length, dtype=jnp.int32)
    frequency = jnp.where(column <= half_length, column, column - half_length)
    low_count = 64
    high_count = length // low_count
    low = jnp.arange(low_count, dtype=jnp.int32)
    high = jnp.arange(high_count, dtype=jnp.int32) * low_count
    scale = 2.0 * math.pi / length
    low_angle = scale * (low[:, None] * frequency[None, :] % length).astype(jnp.float32)
    high_angle = scale * (high[:, None] * frequency[None, :] % length).astype(jnp.float32)
    low_cos, low_sin = (jnp.cos(low_angle), jnp.sin(low_angle))
    high_cos, high_sin = (jnp.cos(high_angle), jnp.sin(high_angle))
    cos_part = high_cos[:, None] * low_cos[None] - high_sin[:, None] * low_sin[None]
    sin_part = high_sin[:, None] * low_cos[None] + high_cos[:, None] * low_sin[None]
    basis = jnp.where((column <= half_length)[None, None, :], cos_part, sin_part)
    return basis.reshape(length, length)


def polar_filter(values, band_rows):
    fields, levels, rows, block_cells = values.shape
    parts = lax.axis_size("lon")
    length = block_cells * parts
    flat = values.reshape(fields * levels * rows, block_cells)
    circles = lax.all_to_all(flat, "lon", split_axis=0, concat_axis=1, tiled=True)
    basis_table = circle_basis(length)
    spectrum = jnp.dot(circles, basis_table, precision=PRECISE)
    factors = column_factors(band_rows, length)
    circle_rows = circles.shape[0]
    scaled = (spectrum.reshape(circle_rows // rows, rows, length) * factors[None]).reshape(
        circle_rows, length
    )
    change = lax.dot_general(scaled, basis_table, (((1,), (1,)), ((), ())), precision=PRECISE)
    back = lax.all_to_all(change, "lon", split_axis=1, concat_axis=0, tiled=True)
    return values + back.reshape(values.shape)


def departure_terms(tracers, dep_owner, dep_row, dep_weight):
    band_count = lax.axis_size("lat")
    row_count, link_count = dep_owner.shape
    entries = row_count * link_count
    capacity = max(2, -(-2 * entries // band_count))
    owner_ids = dep_owner.reshape(entries)
    source = dep_row.reshape(entries)
    positions = jnp.arange(entries)
    earlier = (owner_ids[:, None] == owner_ids[None, :]) & (positions[None, :] < positions[:, None])
    slot_ids = jnp.sum(earlier.astype(jnp.int32), axis=1)
    band_ids = jnp.arange(band_count, dtype=jnp.int32)
    slot_range = jnp.arange(capacity, dtype=jnp.int32)
    matches = (owner_ids[:, None, None] == band_ids[None, :, None]) & (
        slot_ids[:, None, None] == slot_range[None, None, :]
    )
    request = jnp.sum(jnp.where(matches, source[:, None, None], 0), axis=0)
    wanted = lax.all_to_all(request, "lat", split_axis=0, concat_axis=0, tiled=True)
    by_row = jnp.transpose(tracers, (2, 0, 1, 3))
    outgoing = by_row[wanted]
    incoming = lax.all_to_all(outgoing, "lat", split_axis=0, concat_axis=0, tiled=True)
    stacked_rows = incoming.reshape((band_count * capacity,) + incoming.shape[2:])
    picked = stacked_rows[owner_ids * capacity + slot_ids].reshape(
        (row_count, link_count) + stacked_rows.shape[1:]
    )
    summed = dep_weight[:, 0][:, None, None, None] * picked[:, 0]
    summed = summed + dep_weight[:, 1][:, None, None, None] * picked[:, 1]
    return jnp.transpose(summed, (1, 2, 0, 3))


def body(
    prognostic,
    tracers,
    zonal_courant,
    meridional_courant,
    filter_band,
    dep_owner,
    dep_row,
    dep_weight,
):
    row_count = prognostic.shape[2]
    departed = departure_terms(tracers, dep_owner, dep_row, dep_weight)
    lon_padded = padded(
        jnp.concatenate([prognostic, zonal_courant[None]], axis=0), (("lon", 3),), 1, True
    )
    zonal_flux = face_flux(lon_padded[:-1], lon_padded[-1:], 3)
    lat_padded = padded(
        jnp.concatenate([prognostic, meridional_courant[None]], axis=0), (("lat", 2),), 1, False
    )
    merid_flux = face_flux(lat_padded[:-1], lat_padded[-1:], 2)
    total_rows = row_count * lax.axis_size("lat")
    face_rows = lax.axis_index("lat") * row_count + jnp.arange(row_count + 1) - 1
    merid_flux = jnp.where(
        (face_rows == total_rows - 1)[None, None, :, None], jnp.float32(0.0), merid_flux
    )
    advected = (
        prognostic
        - (zonal_flux[..., 1:] - zonal_flux[..., :-1])
        - (merid_flux[:, :, 1:] - merid_flux[:, :, :-1])
    )
    new_prognostic = polar_filter(advected, filter_band)
    return (new_prognostic, departed)


def solution(mesh):
    return jax.shard_map(
        body,
        mesh=mesh,
        in_specs=(
            P(None, None, "lat", "lon"),
            P(None, None, "lat", "lon"),
            P(None, "lat", "lon"),
            P(None, "lat", "lon"),
            P("lat"),
            P("lat", None),
            P("lat", None),
            P("lat", None),
        ),
        out_specs=(P(None, None, "lat", "lon"), P(None, None, "lat", "lon")),
        check_vma=False,
    )
```

profile of v0, /device:TPU:0, one launch (start us, length us, event | category | flops | bytes accessed | tf_op | source)
XLA Modules:
  0.0 364.4 jit_solution(3108932577473310589)
XLA Ops:
  0.7 3.3 pad_maximum_fusion.8
  10.8 4.9 %collective-permute-start.2 = (f32[5,16,1,384]{3,1,2,0:T(8,128)}, f32[5,16,1,384]{3,1,2,0:T(8,128)}, u32[]{:S(2)}, u32[]{:S(2)}) collective-permute-start(f32[5,16,1,384]{3,1,2,0:T(8,128)} %copy.61), channel_id=1, source_target_pairs={{0,1},{1,2},{2,3},{3,4},{4,5},{5,6},{6,7},{8,9},{9,10},{10,11},{11... | collective-permute-start | bytes 368648 | tf_op jit(solution)/shard_map/ppermute | solution.py:17
  20.8 2.2 multiply_bitcast_fusion.1
  24.0 2.3 copy.60
  26.3 2.7 multiply_subtract_fusion
  32.6 2.3 fusion.4
  34.9 3.6 all-to-all-start
  41.5 5.8 %add_select_fusion = f32[24,64,1536]{2,1,0:T(8,128)} fusion(f32[64,1536]{1,0:T(8,128)S(1)} %get-tuple-element.21, f32[24,1536]{1,0:T(8,128)S(1)} %get-tuple-element.19, f32[64,1536]{1,0:T(8,128)S(1)} %get-tuple-element.20, f32[24,1536]{1,0:T(8,128)S(1)} %get-tuple-element.18, pred[1536]{0:T(1024)(128)(4,1)S(1)} %iota_compare_fusion.4), kind=kLoop, calls=%fused_computation.2 | loop fusion | flops 16515072 | bytes 10520064 | tf_op jit(solution)/shard_map/jit(_where)/select_n | solution.py:62
  47.3 19.7 %all-to-all-done = f32[4,384,384]{2,1,0:T(8,128)S(1)} async-done(((f32[4,384,384]{2,1,0:T(8,128)}), f32[4,384,384]{2,1,0:T(8,128)S(1)}, u32[]{:S(2)}, u32[]{:S(2)}) %all-to-all-start) | async-done | bytes 2359328 | tf_op jit(solution)/shard_map/all_to_all | solution.py:71
  67.0 6.9 %all-to-all-start.2 = ((s32[8,1,12]{2,1,0:T(1,128)}), s32[8,1,12]{2,1,0:T(1,128)S(1)}, u32[]{:S(2)}, u32[]{:S(2)}) async-start(s32[8,1,12]{2,1,0:T(1,128)} %copy.70), calls=%async_computation.2 | async-start | bytes 8192 | tf_op jit(solution)/shard_map/all_to_all | solution.py:100
  73.9 2.9 copy.65
  76.9 2.7 dot_general.8
  79.6 14.7 %convolution_multiply_fusion = f32[16,24,1536]{2,1,0:T(8,128)S(1)} fusion(f32[16,24,1536]{2,1,0:T(8,128)S(1)} %dot_general.8, f32[1536,1536,1]{1,0,2:T(8,128)} %bitcast.64, f32[24,1536]{1,0:T(8,128)S(1)} %fusion.18), kind=kOutput, calls=%fused_computation.13 | convolution fusion | flops 10872225792 | bytes 14303232 | tf_op jit(solution)/shard_map/dot_general | solution.py:73
  94.3 13.0 %fusion.31 = f32[384,4,384]{2,0,1:T(8,128)} fusion(f32[384,1536,1]{1,0,2:T(8,128)S(1)} %bitcast.71, f32[4,384,1536]{2,1,0:T(8,128)S(1)} %bitcast.65), kind=kOutput, calls=%fused_computation.87 | convolution fusion | flops 10871635968 | bytes 14155776 | tf_op jit(solution)/shard_map/dot_general | solution.py:79
  107.3 4.8 %all-to-all-start.1 = ((f32[384,4,384]{2,0,1:T(8,128)}), f32[384,4,384]{2,0,1:T(8,128)}, u32[]{:S(2)}, u32[]{:S(2)}) async-start(f32[384,4,384]{2,0,1:T(8,128)} %fusion.31), calls=%async_computation.1 | async-start | bytes 4718592 | tf_op jit(solution)/shard_map/all_to_all | solution.py:80
  112.1 2.1 copy.78
  114.3 4.8 %gather_fusion = f32[96,4,16,384]{3,2,1,0:T(8,128)} fusion(f32[24,4,16,384]{3,2,1,0:T(8,128)S(1)} %bitcast.66, s32[1024]{0:T(1024)S(1)} %pad_clamp_fusion.1), kind=kCustom, calls=%fused_computation | custom fusion | bytes 18874752 | tf_op jit(solution)/shard_map/gather | solution.py:102
  119.1 21.3 %all-to-all-done.1 = f32[384,4,384]{2,0,1:T(8,128)} async-done(((f32[384,4,384]{2,0,1:T(8,128)}), f32[384,4,384]{2,0,1:T(8,128)}, u32[]{:S(2)}, u32[]{:S(2)}) %all-to-all-start.1) | async-done | bytes 2359328 | tf_op jit(solution)/shard_map/all_to_all | solution.py:80
  140.4 6.1 %all-to-all-start.3 = ((f32[8,12,4,16,384]{4,3,2,1,0:T(8,128)}), f32[8,12,4,16,384]{4,3,2,1,0:T(8,128)}, u32[]{:S(2)}, u32[]{:S(2)}) async-start(f32[8,12,4,16,384]{4,3,2,1,0:T(8,128)} %bitcast.67), calls=%async_computation.3 | async-start | bytes 18874368 | tf_op jit(solution)/shard_map/all_to_all | solution.py:103
  146.8 3.3 add.134
  150.1 201.9 %all-to-all-done.3 = f32[8,12,4,16,384]{4,3,2,1,0:T(8,128)} async-done(((f32[8,12,4,16,384]{4,3,2,1,0:T(8,128)}), f32[8,12,4,16,384]{4,3,2,1,0:T(8,128)}, u32[]{:S(2)}, u32[]{:S(2)}) %all-to-all-start.3) | async-done | bytes 9437216 | tf_op jit(solution)/shard_map/all_to_all | solution.py:103
  352.0 6.7 %gather_fusion.1 = f32[48,4,16,384]{3,2,1,0:T(8,128)} fusion(f32[96,4,16,384]{3,2,1,0:T(8,128)} %bitcast.20, s32[1024]{0:T(1024)S(1)} %pad_clamp_fusion), kind=kCustom, calls=%fused_computation.1 | custom fusion | bytes 9437376 | tf_op jit(solution)/shard_map/gather | solution.py:105
  358.7 2.9 fusion.2
  361.6 2.8 copy.73
  (72 shorter events, 19.6 us)
Async XLA Ops:
  0.6 9.3 %copy-start = (f32[4,16,24,384]{3,2,1,0:T(8,128)S(1)}, f32[4,16,24,384]{3,2,1,0:T(8,128)}, u32[]{:S(2)}) copy-start(f32[4,16,24,384]{3,2,1,0:T(8,128)} %param.8) | copy-start | bytes 7077892
  0.6 9.3 %copy-start.3 = (f32[16,24,384]{2,1,0:T(8,128)S(1)}, f32[16,24,384]{2,1,0:T(8,128)}, u32[]{:S(2)}) copy-start(f32[16,24,384]{2,1,0:T(8,128)} %param.11) | copy-start | bytes 1769476
  4.0 13.7 %copy-start.5 = (s32[24,2]{0,1:T(2,128)S(1)}, s32[24,2]{0,1:T(2,128)}, u32[]{:S(2)}) copy-start(s32[24,2]{0,1:T(2,128)} %param.13) | copy-start | bytes 580
  4.0 14.1 %copy-start.11 = (s32[24]{0:T(128)S(1)}, s32[24]{0:T(128)}, u32[]{:S(2)}) copy-start(s32[24]{0:T(128)} %param.12) | copy-start | bytes 292
  4.0 14.1 %copy-start.7 = (s32[24,2]{0,1:T(2,128)S(1)}, s32[24,2]{0,1:T(2,128)}, u32[]{:S(2)}) copy-start(s32[24,2]{0,1:T(2,128)} %param.14) | copy-start | bytes 580
  5.7 13.8 %collective-permute-start = (f32[5,16,24,1]{2,1,3,0:T(8,128)S(1)}, f32[5,16,24,1]{2,1,3,0:T(8,128)}, u32[]{:S(2)}, u32[]{:S(2)}) collective-permute-start(f32[5,16,24,1]{2,1,3,0:T(8,128)S(1)} %copy.57), channel_id=1, source_target_pairs={{0,8},{8,16},{16,24},{24,0},{1,9},{9,17},{17,25},{25,1},{2,10},{10... | collective-permute-start | bytes 23048 | tf_op jit(solution)/shard_map/ppermute | solution.py:17
  7.9 16.1 %collective-permute-start.1 = (f32[5,16,24,1]{2,1,3,0:T(8,128)S(1)}, f32[5,16,24,1]{2,1,3,0:T(8,128)}, u32[]{:S(2)}, u32[]{:S(2)}) collective-permute-start(f32[5,16,24,1]{2,1,3,0:T(8,128)S(1)} %copy.59), channel_id=1, source_target_pairs={{8,0},{16,8},{24,16},{0,24},{9,1},{17,9},{25,17},{1,25},{10,2},{18... | collective-permute-start | bytes 23048 | tf_op jit(solution)/shard_map/ppermute | solution.py:18
  10.8 18.3 %collective-permute-start.2 = (f32[5,16,1,384]{3,1,2,0:T(8,128)}, f32[5,16,1,384]{3,1,2,0:T(8,128)}, u32[]{:S(2)}, u32[]{:S(2)}) collective-permute-start(f32[5,16,1,384]{3,1,2,0:T(8,128)} %copy.61), channel_id=1, source_target_pairs={{0,1},{1,2},{2,3},{3,4},{4,5},{5,6},{6,7},{8,9},{9,10},{10,11},{11... | collective-permute-start | bytes 368648 | tf_op jit(solution)/shard_map/ppermute | solution.py:17
  16.3 14.1 %collective-permute-start.3 = (f32[5,16,1,384]{3,1,2,0:T(8,128)}, f32[5,16,1,384]{3,1,2,0:T(8,128)}, u32[]{:S(2)}, u32[]{:S(2)}) collective-permute-start(f32[5,16,1,384]{3,1,2,0:T(8,128)} %copy.63), channel_id=1, source_target_pairs={{1,0},{2,1},{3,2},{4,3},{5,4},{6,5},{7,6},{9,8},{10,9},{11,10},{12... | collective-permute-start | bytes 368648 | tf_op jit(solution)/shard_map/ppermute | solution.py:18
  18.0 0.6 copy-start.9
  26.3 3.8 %copy-start.4 = (f32[16,24,384]{2,1,0:T(8,128)S(1)}, f32[16,24,384]{2,1,0:T(8,128)}, u32[]{:S(2)}) copy-start(f32[16,24,384]{2,1,0:T(8,128)} %param.11) | copy-start | bytes 1769476
  30.1 1.3 copy-start.8
  34.9 32.1 %all-to-all-start = ((f32[4,384,384]{2,1,0:T(8,128)}), f32[4,384,384]{2,1,0:T(8,128)S(1)}, u32[]{:S(2)}, u32[]{:S(2)}) async-start(f32[4,384,384]{2,1,0:T(8,128)} %bitcast.68), calls=%async_computation | async-start | bytes 4718592 | tf_op jit(solution)/shard_map/all_to_all | solution.py:71
  67.0 40.3 %all-to-all-start.2 = ((s32[8,1,12]{2,1,0:T(1,128)}), s32[8,1,12]{2,1,0:T(1,128)S(1)}, u32[]{:S(2)}, u32[]{:S(2)}) async-start(s32[8,1,12]{2,1,0:T(1,128)} %copy.70), calls=%async_computation.2 | async-start | bytes 8192 | tf_op jit(solution)/shard_map/all_to_all | solution.py:100
  79.6 14.8 %copy-start.1 = (f32[24,64,1536]{2,1,0:T(8,128)S(1)}, f32[24,64,1536]{2,1,0:T(8,128)}, u32[]{:S(2)}) copy-start(f32[24,64,1536]{2,1,0:T(8,128)} %add_select_fusion) | copy-start | bytes 28311556
  107.3 33.1 %all-to-all-start.1 = ((f32[384,4,384]{2,0,1:T(8,128)}), f32[384,4,384]{2,0,1:T(8,128)}, u32[]{:S(2)}, u32[]{:S(2)}) async-start(f32[384,4,384]{2,0,1:T(8,128)} %fusion.31), calls=%async_computation.1 | async-start | bytes 4718592 | tf_op jit(solution)/shard_map/all_to_all | solution.py:80
  140.4 6.3 %copy-start.10 = (s32[48]{0:T(128)S(1)}, s32[48]{0:T(128)}, u32[]{:S(2)}) copy-start(s32[48]{0:T(128)} %copy-done.9) | copy-start | bytes 580
  140.4 6.4 %copy-start.6 = (f32[24,2]{0,1:T(2,128)S(1)}, f32[24,2]{0,1:T(2,128)}, u32[]{:S(2)}) copy-start(f32[24,2]{0,1:T(2,128)} %param.15) | copy-start | bytes 580
  140.4 6.4 %copy-start.2 = (f32[4,16,24,384]{3,2,1,0:T(8,128)S(1)}, f32[4,16,24,384]{3,2,1,0:T(8,128)}, u32[]{:S(2)}) copy-start(f32[4,16,24,384]{3,2,1,0:T(8,128)} %fusion.4) | copy-start | bytes 7077892
  140.4 211.6 %all-to-all-start.3 = ((f32[8,12,4,16,384]{4,3,2,1,0:T(8,128)}), f32[8,12,4,16,384]{4,3,2,1,0:T(8,128)}, u32[]{:S(2)}, u32[]{:S(2)}) async-start(f32[8,12,4,16,384]{4,3,2,1,0:T(8,128)} %bitcast.67), calls=%async_computation.3 | async-start | bytes 18874368 | tf_op jit(solution)/shard_map/all_to_all | solution.py:103
where the time goes:
time: 365 us; the launch traced here: 364 us
  waiting for transfers between devices  243 us (67%)
  local copies, waits for them, and re-layouts  34.2 us (9%)
  starting transfers between devices  30.1 us (8%)
  other arithmetic  28.6 us (8%)
  matrix products  27.7 us (8%)
    all_to_all x1, waiting for transfers between devices, departure_terms(): lax.all_to_all(outgoing, 'lat', split_axis=0, concat_axis=0, tiled=True)  202 us
    all_to_all x1, waiting for transfers between devices, polar_filter(): lax.all_to_all(change, 'lon', split_axis=1, concat_axis=0, tiled=True)  21.3 us
    all_to_all x1, waiting for transfers between devices, polar_filter(): lax.all_to_all(flat, 'lon', split_axis=0, concat_axis=1, tiled=True)  19.7 us
    dot_general x1, matrix products, polar_filter(): spectrum = jnp.dot(circles, basis_table, precision=PRECISE)  14.7 us
    dot_general x1, matrix products, polar_filter(): lax.dot_general(scaled, basis_table, (((1,), (1,)), ((), ())), precision=...  13 us
  transfers between devices with their start and end apart: 8, of which 3 were waited for; matrix products, arithmetic and copies ran while one was open for 19% of the time, Pallas kernels for 0%

commit v1 on v0

--- a/solution.py
+++ b/solution.py
@@ -77,7 +77,15 @@
         circle_rows, length
     )
     change = lax.dot_general(scaled, basis_table, (((1,), (1,)), ((), ())), precision=PRECISE)
-    back = lax.all_to_all(change, "lon", split_axis=1, concat_axis=0, tiled=True)
+    ways, here = (lax.axis_size("lon"), lax.axis_index("lon"))
+    width_2 = change.shape[1] // ways
+    turned = jnp.roll(change, -here * width_2, axis=1)
+    got = [lax.slice_in_dim(turned, 0, width_2, axis=1)]
+    for far in range(1, ways):
+        sent = lax.slice_in_dim(turned, far * width_2, (far + 1) * width_2, axis=1)
+        got.append(lax.ppermute(sent, "lon", [(d, (d + far) % ways) for d in range(ways)]))
+    line = jnp.concatenate(got[::-1], axis=0)
+    back = jnp.roll(line, (here + 1) * got[0].shape[0], axis=0)
     return values + back.reshape(values.shape)
 
 

time: 365 us -> 298 us (0.82)
  waiting for transfers between devices: 243 us -> 176 us
    all_to_all x1, waiting for transfers between devices: 202 us -> 131 us  [departure_terms(): lax.all_to_all(outgoing, 'lat', split_axis=0, concat_axis=0, tiled=True)]
    ppermute x0 -> x3, waiting for transfers between devices: none -> 24 us  [polar_filter(): lax.ppermute(sent, 'lon', [(d, (d + far) % ways) for d in range(ways)])]
    all_to_all x1 -> x0, waiting for transfers between devices: 21.3 us -> none  [polar_filter(): lax.all_to_all(change, 'lon', split_axis=1, concat_axis=0, tiled=True)]
    all_to_all x1 -> x0, starting transfers between devices: 4.78 us -> none  [polar_filter(): lax.all_to_all(change, 'lon', split_axis=1, concat_axis=0, tiled=True)]
    unnamed x28 -> x31, local copies, waits for them, and re-layouts: 5.44 us -> 7.38 us
  transfers between devices with their start and end apart: 8 -> 10, of which waited for: 3 -> 5; matrix products, arithmetic and copies ran while one was open for 19% -> 25% of each run, Pallas kernels for 0% -> 0%
where the time goes in v1:
time: 298 us; the launch traced here: 297 us
  waiting for transfers between devices  176 us (59%)
  local copies, waits for them, and re-layouts  36.4 us (12%)
  other arithmetic  29.2 us (10%)
  starting transfers between devices  27.2 us (9%)
  matrix products  27.1 us (9%)
    all_to_all x1, waiting for transfers between devices, departure_terms(): lax.all_to_all(outgoing, 'lat', split_axis=0, concat_axis=0, tiled=True)  131 us
    ppermute x3, waiting for transfers between devices, polar_filter(): lax.ppermute(sent, 'lon', [(d, (d + far) % ways) for d in range(ways)])  24 us
    all_to_all x1, waiting for transfers between devices, polar_filter(): lax.all_to_all(flat, 'lon', split_axis=0, concat_axis=1, tiled=True)  21.5 us
    dot_general x1, matrix products, polar_filter(): spectrum = jnp.dot(circles, basis_table, precision=PRECISE)  15.5 us
    dot_general x1, matrix products, polar_filter(): lax.dot_general(scaled, basis_table, (((1,), (1,)), ((), ())), precision=...  11.6 us
    unnamed x31, local copies, waits for them, and re-layouts  7.38 us
    all_to_all x1, starting transfers between devices, departure_terms(): lax.all_to_all(request, 'lat', split_axis=0, concat_axis=0, tiled=True)  6.93 us
    gather x1, local copies, waits for them, and re-layouts, departure_terms(): stacked_rows[owner_ids * capacity + slot_ids]  6.74 us
  transfers between devices with their start and end apart: 10, of which 5 were waited for; matrix products, arithmetic and copies ran while one was open for 25% of the time, Pallas kernels for 0%

profile of v1, /device:TPU:0, one launch (start us, length us, event | category | flops | bytes accessed | tf_op | source)
XLA Modules:
  0.0 297.3 jit_solution(7615266740120763442)
XLA Ops:
  0.7 1.9 pad_maximum_fusion.11
  3.2 5.5 %collective-permute-start.2 = (f32[5,16,1,384]{3,1,2,0:T(8,128)}, f32[5,16,1,384]{3,1,2,0:T(8,128)}, u32[]{:S(2)}, u32[]{:S(2)}) collective-permute-start(f32[5,16,1,384]{3,1,2,0:T(8,128)} %copy.60), channel_id=1, source_target_pairs={{0,1},{1,2},{2,3},{3,4},{4,5},{5,6},{6,7},{8,9},{9,10},{10,11},{11... | collective-permute-start | bytes 368648 | tf_op jit(solution)/shard_map/ppermute | solution.py:17
  11.4 2.4 copy.56
  18.2 6.9 %all-to-all-start.1 = ((s32[8,1,12]{2,1,0:T(1,128)}), s32[8,1,12]{2,1,0:T(1,128)S(1)}, u32[]{:S(2)}, u32[]{:S(2)}) async-start(s32[8,1,12]{2,1,0:T(1,128)} %copy.69), calls=%async_computation.1 | async-start | bytes 8192 | tf_op jit(solution)/shard_map/all_to_all | solution.py:108
  27.0 2.2 multiply_bitcast_fusion.1
  31.7 2.7 multiply_subtract_fusion
  38.0 2.3 fusion.5
  40.3 4.5 %all-to-all-start = ((f32[4,384,384]{2,1,0:T(8,128)}), f32[4,384,384]{2,1,0:T(8,128)}, u32[]{:S(2)}, u32[]{:S(2)}) async-start(f32[4,384,384]{2,1,0:T(8,128)} %bitcast.63), calls=%async_computation | async-start | bytes 4718592 | tf_op jit(solution)/shard_map/all_to_all | solution.py:71
  44.8 2.1 copy.77
  47.0 4.8 %gather_fusion = f32[96,4,16,384]{3,2,1,0:T(8,128)} fusion(f32[24,4,16,384]{3,2,1,0:T(8,128)S(1)} %bitcast.61, s32[1024]{0:T(1024)S(1)} %pad_clamp_fusion.1), kind=kCustom, calls=%fused_computation | custom fusion | bytes 18874752 | tf_op jit(solution)/shard_map/gather | solution.py:110
  51.8 21.5 %all-to-all-done = f32[4,384,384]{2,1,0:T(8,128)} async-done(((f32[4,384,384]{2,1,0:T(8,128)}), f32[4,384,384]{2,1,0:T(8,128)}, u32[]{:S(2)}, u32[]{:S(2)}) %all-to-all-start) | async-done | bytes 2359328 | tf_op jit(solution)/shard_map/all_to_all | solution.py:71
  73.3 6.1 %all-to-all-start.2 = ((f32[8,12,4,16,384]{4,3,2,1,0:T(8,128)}), f32[8,12,4,16,384]{4,3,2,1,0:T(8,128)}, u32[]{:S(2)}, u32[]{:S(2)}) async-start(f32[8,12,4,16,384]{4,3,2,1,0:T(8,128)} %bitcast.62), calls=%async_computation.2 | async-start | bytes 18874368 | tf_op jit(solution)/shard_map/all_to_all | solution.py:111
  81.9 5.8 %add_select_fusion = f32[24,64,1536]{2,1,0:T(8,128)} fusion(f32[64,1536]{1,0:T(8,128)S(1)} %get-tuple-element.24, f32[24,1536]{1,0:T(8,128)S(1)} %get-tuple-element.22, f32[64,1536]{1,0:T(8,128)S(1)} %get-tuple-element.23, f32[24,1536]{1,0:T(8,128)S(1)} %get-tuple-element.21, pred[1536]{0:T(1024)(128)(4,1)S(1)} %iota_compare_fusion.4), kind=kLoop, calls=%fused_computation.2 | loop fusion | flops 16515072 | bytes 10520064 | tf_op jit(solution)/shard_map/jit(_where)/select_n | solution.py:62
  87.8 3.2 %copy.64 = f32[384,4,384]{2,1,0:T(4,128)S(1)} copy(f32[384,4,384]{2,0,1:T(8,128)} %bitcast.7) | data formatting | bytes 4718592 | tf_op jit(solution)/shard_map/all_to_all | solution.py:71
  90.9 2.0 dot_general.8
  92.9 15.5 %convolution_multiply_fusion = f32[16,24,1536]{2,1,0:T(8,128)S(1)} fusion(f32[16,24,1536]{2,1,0:T(8,128)} %dot_general.8, f32[1536,1536,1]{1,0,2:T(8,128)} %bitcast.59, f32[24,1536]{1,0:T(8,128)S(1)} %fusion.19), kind=kOutput, calls=%fused_computation.15 | convolution fusion | flops 10872225792 | bytes 14303232 | tf_op jit(solution)/shard_map/dot_general | solution.py:73
  108.4 11.6 %fusion.33 = f32[384,1536]{1,0:T(8,128)S(1)} fusion(f32[384,1536]{1,0:T(8,128)S(1)} %bitcast.66, f32[1536,1536]{1,0:T(8,128)S(1)} %bitcast.60), kind=kOutput, calls=%fused_computation.100 | convolution fusion | flops 10871635968 | bytes 14155776 | tf_op jit(solution)/shard_map/dot_general | solution.py:79
  126.4 8.7 %collective-permute-done.4 = f32[384,384]{1,0:T(8,128)S(1)} collective-permute-done((f32[384,384]{1,0:T(8,128)}, f32[384,384]{1,0:T(8,128)S(1)}, u32[]{:S(2)}, u32[]{:S(2)}) %collective-permute-start.4) | collective-permute-done | bytes 589856 | tf_op jit(solution)/shard_map/ppermute | solution.py:86
  135.1 13.2 %collective-permute-done.5 = f32[384,384]{1,0:T(8,128)S(1)} collective-permute-done((f32[384,384]{1,0:T(8,128)}, f32[384,384]{1,0:T(8,128)S(1)}, u32[]{:S(2)}, u32[]{:S(2)}) %collective-permute-start.5) | collective-permute-done | bytes 589856 | tf_op jit(solution)/shard_map/ppermute | solution.py:86
  148.4 2.1 collective-permute-done.6
  154.1 130.8 %all-to-all-done.2 = f32[8,12,4,16,384]{4,3,2,1,0:T(8,128)} async-done(((f32[8,12,4,16,384]{4,3,2,1,0:T(8,128)}), f32[8,12,4,16,384]{4,3,2,1,0:T(8,128)}, u32[]{:S(2)}, u32[]{:S(2)}) %all-to-all-start.2) | async-done | bytes 9437216 | tf_op jit(solution)/shard_map/all_to_all | solution.py:111
  284.9 6.7 %gather_fusion.1 = f32[48,4,16,384]{3,2,1,0:T(8,128)} fusion(f32[96,4,16,384]{3,2,1,0:T(8,128)} %bitcast.17, s32[1024]{0:T(1024)S(1)} %pad_clamp_fusion), kind=kCustom, calls=%fused_computation.1 | custom fusion | bytes 9437376 | tf_op jit(solution)/shard_map/gather | solution.py:113
  291.6 2.9 fusion.3
  294.5 2.8 copy.72
  (83 shorter events, 27.9 us)
Async XLA Ops:
  0.6 9.4 %copy-start = (f32[4,16,24,384]{3,2,1,0:T(8,128)S(1)}, f32[4,16,24,384]{3,2,1,0:T(8,128)}, u32[]{:S(2)}) copy-start(f32[4,16,24,384]{3,2,1,0:T(8,128)} %param.8) | copy-start | bytes 7077892
  0.6 9.4 %copy-start.3 = (f32[16,24,384]{2,1,0:T(8,128)S(1)}, f32[16,24,384]{2,1,0:T(8,128)}, u32[]{:S(2)}) copy-start(f32[16,24,384]{2,1,0:T(8,128)} %param.10) | copy-start | bytes 1769476
  3.2 31.2 %collective-permute-start.2 = (f32[5,16,1,384]{3,1,2,0:T(8,128)}, f32[5,16,1,384]{3,1,2,0:T(8,128)}, u32[]{:S(2)}, u32[]{:S(2)}) collective-permute-start(f32[5,16,1,384]{3,1,2,0:T(8,128)} %copy.60), channel_id=1, source_target_pairs={{0,1},{1,2},{2,3},{3,4},{4,5},{5,6},{6,7},{8,9},{9,10},{10,11},{11... | collective-permute-start | bytes 368648 | tf_op jit(solution)/shard_map/ppermute | solution.py:17
  8.7 27.0 %collective-permute-start.3 = (f32[5,16,1,384]{3,1,2,0:T(8,128)S(1)}, f32[5,16,1,384]{3,1,2,0:T(8,128)}, u32[]{:S(2)}, u32[]{:S(2)}) collective-permute-start(f32[5,16,1,384]{3,1,2,0:T(8,128)S(1)} %copy.62), channel_id=1, source_target_pairs={{1,0},{2,1},{3,2},{4,3},{5,4},{6,5},{7,6},{9,8},{10,9},{11,10},{12... | collective-permute-start | bytes 368648 | tf_op jit(solution)/shard_map/ppermute | solution.py:18
  10.1 6.0 %copy-start.5 = (s32[24,2]{0,1:T(2,128)S(1)}, s32[24,2]{0,1:T(2,128)}, u32[]{:S(2)}) copy-start(s32[24,2]{0,1:T(2,128)} %param.13) | copy-start | bytes 580
  10.1 6.9 %copy-start.6 = (s32[24,2]{0,1:T(2,128)S(1)}, s32[24,2]{0,1:T(2,128)}, u32[]{:S(2)}) copy-start(s32[24,2]{0,1:T(2,128)} %param.14) | copy-start | bytes 580
  13.7 11.9 %collective-permute-start = (f32[5,16,24,1]{2,1,3,0:T(8,128)}, f32[5,16,24,1]{2,1,3,0:T(8,128)}, u32[]{:S(2)}, u32[]{:S(2)}) collective-permute-start(f32[5,16,24,1]{2,1,3,0:T(8,128)} %copy.56), channel_id=1, source_target_pairs={{0,8},{8,16},{16,24},{24,0},{1,9},{9,17},{17,25},{25,1},{2,10},{10... | collective-permute-start | bytes 23048 | tf_op jit(solution)/shard_map/ppermute | solution.py:17
  14.2 15.9 %collective-permute-start.1 = (f32[5,16,24,1]{2,1,3,0:T(8,128)S(1)}, f32[5,16,24,1]{2,1,3,0:T(8,128)S(1)}, u32[]{:S(2)}, u32[]{:S(2)}) collective-permute-start(f32[5,16,24,1]{2,1,3,0:T(8,128)S(1)} %copy.58), channel_id=1, source_target_pairs={{8,0},{16,8},{24,16},{0,24},{9,1},{17,9},{25,17},{1,25},{10,2},{18... | collective-permute-start | bytes 23048 | tf_op jit(solution)/shard_map/ppermute | solution.py:18
  16.4 0.6 copy-start.8
  18.2 22.1 %all-to-all-start.1 = ((s32[8,1,12]{2,1,0:T(1,128)}), s32[8,1,12]{2,1,0:T(1,128)S(1)}, u32[]{:S(2)}, u32[]{:S(2)}) async-start(s32[8,1,12]{2,1,0:T(1,128)} %copy.69), calls=%async_computation.1 | async-start | bytes 8192 | tf_op jit(solution)/shard_map/all_to_all | solution.py:108
  31.6 3.8 %copy-start.4 = (f32[16,24,384]{2,1,0:T(8,128)S(1)}, f32[16,24,384]{2,1,0:T(8,128)}, u32[]{:S(2)}) copy-start(f32[16,24,384]{2,1,0:T(8,128)} %param.11) | copy-start | bytes 1769476
  35.5 1.3 copy-start.7
  40.3 33.1 %all-to-all-start = ((f32[4,384,384]{2,1,0:T(8,128)}), f32[4,384,384]{2,1,0:T(8,128)}, u32[]{:S(2)}, u32[]{:S(2)}) async-start(f32[4,384,384]{2,1,0:T(8,128)} %bitcast.63), calls=%async_computation | async-start | bytes 4718592 | tf_op jit(solution)/shard_map/all_to_all | solution.py:71
  73.3 6.1 %copy-start.9 = (s32[24]{0:T(128)S(1)}, s32[24]{0:T(128)}, u32[]{:S(2)}) copy-start(s32[24]{0:T(128)} %param.12) | copy-start | bytes 292
  73.3 211.6 %all-to-all-start.2 = ((f32[8,12,4,16,384]{4,3,2,1,0:T(8,128)}), f32[8,12,4,16,384]{4,3,2,1,0:T(8,128)}, u32[]{:S(2)}, u32[]{:S(2)}) async-start(f32[8,12,4,16,384]{4,3,2,1,0:T(8,128)} %bitcast.62), calls=%async_computation.2 | async-start | bytes 18874368 | tf_op jit(solution)/shard_map/all_to_all | solution.py:111
  92.9 15.5 %copy-start.1 = (f32[24,64,1536]{2,1,0:T(8,128)S(1)}, f32[24,64,1536]{2,1,0:T(8,128)}, u32[]{:S(2)}) copy-start(f32[24,64,1536]{2,1,0:T(8,128)} %add_select_fusion) | copy-start | bytes 28311556
  122.5 12.6 %collective-permute-start.4 = (f32[384,384]{1,0:T(8,128)}, f32[384,384]{1,0:T(8,128)S(1)}, u32[]{:S(2)}, u32[]{:S(2)}) collective-permute-start(f32[384,384]{1,0:T(8,128)} %get-tuple-element.20), channel_id=1, source_target_pairs={{0,24},{8,0},{16,8},{24,16},{1,25},{9,1},{17,9},{25,17},{2,26},{10... | collective-permute-start | bytes 1769480 | tf_op jit(solution)/shard_map/ppermute | solution.py:86
  123.9 24.5 %collective-permute-start.5 = (f32[384,384]{1,0:T(8,128)}, f32[384,384]{1,0:T(8,128)S(1)}, u32[]{:S(2)}, u32[]{:S(2)}) collective-permute-start(f32[384,384]{1,0:T(8,128)} %get-tuple-element.19), channel_id=1, source_target_pairs={{0,16},{8,24},{16,0},{24,8},{1,17},{9,25},{17,1},{25,9},{2,18},{10... | collective-permute-start | bytes 1769480 | tf_op jit(solution)/shard_map/ppermute | solution.py:86
  125.6 24.9 %collective-permute-start.6 = (f32[384,384]{1,0:T(8,128)S(1)}, f32[384,384]{1,0:T(8,128)S(1)}, u32[]{:S(2)}, u32[]{:S(2)}) collective-permute-start(f32[384,384]{1,0:T(8,128)S(1)} %get-tuple-element.18), channel_id=1, source_target_pairs={{0,8},{8,16},{16,24},{24,0},{1,9},{9,17},{17,25},{25,1},{2,10},{10... | collective-permute-start | bytes 1769480 | tf_op jit(solution)/shard_map/ppermute | solution.py:86
  150.8 1.7 copy-start.2
